TPU v7x, 256 devices: a whole 4x4x8 slice. The times are simulated.
256 devices in a mesh: sub: 64 (over z, x, core), harm: 4 (over y).
Axes of the slice: x: 4, y: 4, z: 8, core: 2. Of those that a mesh axis runs over, the one named last changes fastest.
Arguments:
- right_side: float32 [16, 128, 16384], P(None, None, 'sub'), may hold values from -6 to 6
- border_side: float32 [16, 128, 2048], P(None, None, 'sub'), may hold values from -6 to 6
- precond_tiles: bfloat16 [32768, 128, 128], P('sub', 'harm'), may hold values from -0.375 to 0.375
- tile_out: int32 [32768], P('sub'), may hold values from 0 to 255
- tile_in: int32 [32768], P('sub'), may hold values from 0 to 255
- couple_tiles: bfloat16 [16384, 128, 128], P('sub', 'harm'), may hold values from -0.1875 to 0.1875
- return_tiles: bfloat16 [16384, 128, 128], P('sub', 'harm'), may hold values from -0.5 to 0.5
- couple_node: int32 [16384], P('sub'), may hold values from 0 to 255
- border_owner: int32 [16384, 1], P('sub'), may hold values from 0 to 63; in each aligned block of 256 rows (0 to 255, 256 to 511, ...) at most 8 rows name the same one
- border_row: int32 [16384], P('sub'), may hold values from 0 to 31
- border_inverse: bfloat16 [2048, 128, 128], P('sub', 'harm'), may hold values from -0.5 to 0.5
Outputs:
- interior_update: float32 [16, 128, 16384], P(None, 'harm', 'sub')
- border_update: float32 [16, 128, 2048], P(None, 'harm', 'sub')
Inputs may be any that keep to these rules, and one draw needn't show every extreme that they name: `border_owner`: among the rows of one subcircuit at most 8 name one owner, a bound that some block reaches of them.
All inputs are finite; a program needn't handle non-finite values.
Results may differ from a plain program's by a relative error of at most 0.005.
Values may be sent and summed in bfloat16 or wider, within the bound.
No kernel may reach another device: no remote copies, remote signals or barrier semaphores. Data moves between devices by JAX's collectives and lax.ppermute only.
A program may use at most 128 MiB of HBM per device.

v0:
```python
import jax
import jax.numpy as jnp
from jax import lax
from jax.sharding import PartitionSpec as P


def collect(values, targets, row_total, first_row=0):
    marks = (
        first_row + jnp.arange(row_total, dtype=jnp.int32)[:, None] == targets[None, :]
    ).astype(jnp.float32)
    flat_rows = values.reshape(values.shape[0], -1)
    summed = jnp.dot(
        marks, flat_rows, precision=lax.Precision.HIGHEST, preferred_element_type=jnp.float32
    )
    return summed.reshape((row_total,) + values.shape[1:])


def tile_product(tile_set, columns, targets, segment_total):
    product = jnp.einsum("tok,trk->tro", tile_set, columns, preferred_element_type=jnp.float32)
    return collect(product, targets, segment_total)


def on_device(
    right_side,
    border_side,
    precond_tiles,
    tile_out,
    tile_in,
    couple_tiles,
    return_tiles,
    couple_node,
    border_owner,
    border_row,
    border_inverse,
):
    harm_block = precond_tiles.shape[1]
    node_count = right_side.shape[2]
    row_count = border_side.shape[2]
    touch_count = couple_node.shape[0]
    sub_count = lax.axis_size("sub")
    harm_offset = lax.axis_index("harm") * harm_block
    side_nodes = jnp.transpose(right_side, (2, 0, 1))
    border_nodes = jnp.transpose(border_side, (2, 0, 1))
    own_border = lax.dynamic_slice_in_dim(border_nodes, harm_offset, harm_block, 2)
    own_side = lax.dynamic_slice_in_dim(side_nodes, harm_offset, harm_block, 2)
    side_low = side_nodes.astype(jnp.bfloat16)
    first_pass = tile_product(precond_tiles, side_low[tile_in], tile_out, node_count).astype(
        jnp.bfloat16
    )
    first_full = lax.all_gather(first_pass, "harm", axis=2, tiled=True)
    partials = jnp.einsum(
        "tok,trk->tro", couple_tiles, first_full[couple_node], preferred_element_type=jnp.float32
    )
    owner_list = border_owner[:, 0]
    value_shape = partials.shape[1:]
    capacity = min(touch_count, max(4, 2 * touch_count // sub_count))
    owner_marks = (owner_list[:, None] == jnp.arange(sub_count, dtype=jnp.int32)[None, :]).astype(
        jnp.int32
    )
    earlier = jnp.cumsum(owner_marks, axis=0) - owner_marks
    slot_index = owner_list * capacity + jnp.sum(earlier * owner_marks, axis=1)
    slot_place = jnp.arange(sub_count * capacity, dtype=jnp.int32)[:, None] == slot_index[None, :]
    place_float = slot_place.astype(jnp.float32)
    send_values = jnp.dot(
        place_float,
        partials.reshape(touch_count, -1),
        precision=lax.Precision.HIGHEST,
        preferred_element_type=jnp.float32,
    )
    send_rows = jnp.sum(slot_place.astype(jnp.int32) * border_row[None, :], axis=1)
    send_values = send_values.reshape((sub_count, capacity) + value_shape)
    send_rows = send_rows.reshape((sub_count, capacity))
    arrived, arrived_rows = (
        lax.all_to_all(send_values, "sub", split_axis=0, concat_axis=0, tiled=True),
        lax.all_to_all(send_rows, "sub", split_axis=0, concat_axis=0, tiled=True),
    )
    incoming = collect(
        arrived.reshape((sub_count * capacity,) + value_shape), arrived_rows.reshape(-1), row_count
    )
    residual_low = (own_border - incoming).astype(jnp.bfloat16)
    residual_full = lax.all_gather(residual_low, "harm", axis=2, tiled=True)
    solved = jnp.einsum(
        "bok,brk->bro", border_inverse, residual_full, preferred_element_type=jnp.float32
    )
    solved, solved_low = (solved, solved.astype(jnp.bfloat16))
    replies = solved_low[arrived_rows]
    returned = lax.all_to_all(replies, "sub", split_axis=0, concat_axis=0, tiled=True)
    returned_flat = returned.reshape(sub_count * capacity, -1)
    touch_low = jnp.dot(
        slot_place.astype(jnp.bfloat16).T, returned_flat, preferred_element_type=jnp.float32
    )
    touch_low = touch_low.astype(jnp.bfloat16).reshape((touch_count,) + value_shape)
    touch_full = lax.all_gather(touch_low, "harm", axis=2, tiled=True)
    correction = tile_product(return_tiles, touch_full, couple_node, node_count)
    update_low = (own_side - correction).astype(jnp.bfloat16)
    update_full = lax.all_gather(update_low, "harm", axis=2, tiled=True)
    second_pass = tile_product(precond_tiles, update_full[tile_in], tile_out, node_count)
    return (jnp.transpose(second_pass, (1, 2, 0)), jnp.transpose(solved, (1, 2, 0)))


def solution(mesh):
    in_specs = (
        P(None, None, "sub"),
        P(None, None, "sub"),
        P("sub", "harm", None),
        P("sub"),
        P("sub"),
        P("sub", "harm", None),
        P("sub", "harm", None),
        P("sub"),
        P("sub", None),
        P("sub"),
        P("sub", "harm", None),
    )
    out_specs = (P(None, "harm", "sub"), P(None, "harm", "sub"))
    return jax.shard_map(
        on_device, mesh=mesh, in_specs=in_specs, out_specs=out_specs, check_vma=False
    )
```

profile of v0, /device:TPU:2, one launch (start us, length us, event | category | flops | bytes accessed | tf_op | source)
XLA Modules:
  0.0 258.4 jit_solution(11936853341196245962)
XLA Ops:
  8.1 2.2 copy.72
  10.3 2.7 %gather_fusion = bf16[512,16,128]{2,1,0:T(8,128)(2,1)} fusion(bf16[256,16,128]{2,1,0:T(8,128)(2,1)S(1)} %bitcast.106, s32[1024]{0:T(1024)S(1)} %pad_clamp_fusion.2), kind=kCustom, calls=%fused_computation | custom fusion | bytes 4196352 | tf_op jit(solution)/shard_map/gather | solution.py:47
  13.0 7.1 %fusion.34 = f32[512,16,32]{2,1,0:T(8,128)} fusion(bf16[512,16,128]{2,1,0:T(8,128)(2,1)} %gather_fusion, bf16[512,32,128]{2,1,0:T(8,128)(2,1)} %param.13), kind=kOutput, calls=%fused_computation.53 | convolution fusion | flops 67108864 | bytes 7340032 | tf_op jit(solution)/shard_map/tok,trk->tro/dot_general | solution.py:19
  20.1 2.8 %copy.73 = f32[512,16,32]{0,2,1:T(8,128)S(1)} copy(f32[512,16,32]{2,1,0:T(8,128)} %fusion.34) | data formatting | bytes 2097152 | tf_op jit(solution)/shard_map/tok,trk->tro/dot_general | solution.py:19
  26.4 12.0 %all-to-all-start = ((s32[64,1,8]{2,1,0:T(1,128)}), s32[64,1,8]{2,1,0:T(1,128)S(1)}, u32[]{:S(2)}, u32[]{:S(2)}) async-start(s32[64,1,8]{2,1,0:T(1,128)} %bitcast.6), calls=%async_computation | async-start | bytes 65536 | tf_op jit(solution)/shard_map/all_to_all | solution.py:75
  38.4 15.9 %all-gather.4.cloned.1.call-done = bf16[256,16,128]{0,1,2:T(8,128)(2,1)} async-done(((bf16[256,16,32]{0,1,2:T(8,128)(2,1)}), bf16[256,16,128]{0,1,2:T(8,128)(2,1)}) %all-gather.4.cloned.1.call-update) | async-done | bytes 1048592 | tf_op jit(solution)/shard_map/all_gather | solution.py:50
  54.3 3.2 %copy.75 = bf16[256,16,128]{2,1,0:T(8,128)(2,1)} copy(bf16[256,16,128]{0,1,2:T(8,128)(2,1)} %all-gather.4.cloned.1.call-done) | data formatting | bytes 2097152 | tf_op jit(solution)/shard_map/all_gather | solution.py:50
  57.5 2.1 gather_fusion.1
  59.5 2.6 fusion.35
  62.1 2.5 copy.76
  64.6 3.4 %fusion.29 = f32[64,16,8,32]{3,2,1,0:T(8,128)} fusion(f32[256,16,32]{0,2,1:T(8,128)S(1)} %copy.76, s32[256]{0:T(256)S(1)} %multiply_add_fusion.1, s32[64,8]{1,0:T(8,128)S(1)} %multiply_add_fusion), kind=kOutput, calls=%fused_computation.52 | convolution fusion | flops 805437440 | bytes 1575936 | tf_op jit(solution)/shard_map/dot_general | solution.py:64
  67.9 4.7 %reshape.169 = f32[64,1,4096]{2,1,0:T(1,128)} reshape(f32[64,16,8,32]{3,2,1,0:T(8,128)} %fusion.29) | data formatting | bytes 2097152
  72.6 10.5 %all-to-all-start.1 = ((f32[64,1,4096]{2,1,0:T(1,128)}), f32[64,1,4096]{2,1,0:T(1,128)S(1)}, u32[]{:S(2)}, u32[]{:S(2)}) async-start(f32[64,1,4096]{2,1,0:T(1,128)} %reshape.169), calls=%async_computation.1 | async-start | bytes 2097152 | tf_op jit(solution)/shard_map/all_to_all | solution.py:74
  84.9 27.1 %all-to-all-done.1 = f32[64,1,4096]{2,1,0:T(1,128)S(1)} async-done(((f32[64,1,4096]{2,1,0:T(1,128)}), f32[64,1,4096]{2,1,0:T(1,128)S(1)}, u32[]{:S(2)}, u32[]{:S(2)}) %all-to-all-start.1) | async-done | bytes 1048608 | tf_op jit(solution)/shard_map/all_to_all | solution.py:74
  112.4 3.3 %reduce.6 = f32[64,4096]{1,0:T(8,128)S(1)} reduce(f32[64,1,4096]{2,1,0:T(1,128)S(1)} %all-to-all-done.1, f32[]{:T(128)} %broadcast.92), dimensions={1}, to_apply=%all_to_all.16.reduce_sub_computation | reduce | bytes 2097156 | tf_op jit(solution)/shard_map/all_to_all | solution.py:74
  115.7 2.7 %reshape.170 = f32[64,16,8,32]{3,2,1,0:T(8,128)} reshape(f32[64,4096]{1,0:T(8,128)S(1)} %reduce.6) | data formatting | bytes 2097152
  118.4 5.1 %copy.77 = f32[64,8,16,32]{3,2,1,0:T(8,128)} copy(f32[64,8,16,32]{3,1,2,0:T(8,128)} %bitcast.105) | data formatting | bytes 2097152 | tf_op jit(solution)/shard_map/all_to_all | solution.py:74
  123.5 3.5 %reshape_reshape.3 = f32[512,512]{1,0:T(8,128)S(1)} reshape(f32[64,8,16,32]{3,2,1,0:T(8,128)} %copy.77) | data formatting | bytes 2097152 | tf_op jit(solution)/shard_map/reshape;reshape | solution.py:11
  129.5 13.3 %all_gather.13 = bf16[32,16,128]{0,1,2:T(8,128)(2,1)S(1)} all-gather(bf16[32,16,32]{0,1,2:T(8,128)(2,1)S(1)} %copy.79), channel_id=1, replica_groups=mesh['sub'=64,'harm'=4] {'harm'}, dimensions={2}, use_global_device_ids=true | all-gather | bytes 163840 | tf_op jit(solution)/shard_map/all_gather | solution.py:81
  143.6 2.8 %gather_fusion.2 = bf16[512,16,32]{2,1,0:T(8,128)(2,1)} fusion(bf16[32,16,32]{2,1,0:T(8,128)(2,1)S(1)} %get-tuple-element.12, s32[1024]{0:T(1024)S(1)} %pad_clamp_fusion), kind=kCustom, calls=%fused_computation.2 | custom fusion | bytes 1050624 | tf_op jit(solution)/shard_map/gather | solution.py:86
  146.4 3.7 %reshape.171 = bf16[64,2,2048]{2,1,0:T(2,128)(2,1)S(1)} reshape(bf16[64,8,16,32]{3,2,1,0:T(8,128)(2,1)} %bitcast.107) | data formatting | bytes 1048576
  150.1 22.9 %all_to_all.22 = bf16[64,2,2048]{2,1,0:T(2,128)(2,1)S(1)} all-to-all(bf16[64,2,2048]{2,1,0:T(2,128)(2,1)S(1)} %reshape.171), channel_id=1, replica_groups=mesh['sub'=64,'harm'=4] {'sub'}, dimensions={0} | all-to-all | bytes 1048576 | tf_op jit(solution)/shard_map/all_to_all | solution.py:87
  174.0 2.1 reshape.114
  177.5 21.9 %all-gather.6.cloned.1.call-done = bf16[256,16,128]{0,1,2:T(8,128)(2,1)} async-done(((bf16[256,16,32]{0,1,2:T(8,128)(2,1)}), bf16[256,16,128]{0,1,2:T(8,128)(2,1)}) %all-gather.6.cloned.1.call-update) | async-done | bytes 1048592 | tf_op jit(solution)/shard_map/all_gather | solution.py:93
  199.4 2.5 copy.83
  201.9 2.8 %fusion.36 = f32[256,16,32]{2,1,0:T(8,128)S(1)} fusion(bf16[256,16,128]{2,1,0:T(8,128)(2,1)S(1)} %copy.83, bf16[256,32,128]{2,1,0:T(8,128)(2,1)} %param.17), kind=kOutput, calls=%fused_computation.55 | convolution fusion | flops 33554432 | bytes 3670016 | tf_op jit(solution)/shard_map/tok,trk->tro/dot_general | solution.py:19
  208.9 26.3 %all-gather.8.cloned.1.call-done = bf16[256,16,128]{0,1,2:T(8,128)(2,1)} async-done(((bf16[256,16,32]{0,1,2:T(8,128)(2,1)}), bf16[256,16,128]{0,1,2:T(8,128)(2,1)}) %all-gather.8.cloned.1.call-update) | async-done | bytes 1048592 | tf_op jit(solution)/shard_map/all_gather | solution.py:96
  235.2 2.5 copy.86
  237.7 2.7 %gather_fusion.3 = bf16[512,16,128]{2,1,0:T(8,128)(2,1)} fusion(bf16[256,16,128]{2,1,0:T(8,128)(2,1)S(1)} %copy.86, s32[1024]{0:T(1024)S(1)} %pad_clamp_fusion.2), kind=kCustom, calls=%fused_computation.3 | custom fusion | bytes 4196352 | tf_op jit(solution)/shard_map/gather | solution.py:97
  240.4 7.1 %fusion.37 = f32[512,16,32]{2,1,0:T(8,128)} fusion(bf16[512,16,128]{2,1,0:T(8,128)(2,1)} %gather_fusion.3, bf16[512,32,128]{2,1,0:T(8,128)(2,1)} %param.13), kind=kOutput, calls=%fused_computation.56 | convolution fusion | flops 67108864 | bytes 7340032 | tf_op jit(solution)/shard_map/tok,trk->tro/dot_general | solution.py:19
  247.5 2.9 %copy.87 = f32[512,16,32]{0,2,1:T(8,128)S(1)} copy(f32[512,16,32]{2,1,0:T(8,128)} %fusion.37) | data formatting | bytes 2097152 | tf_op jit(solution)/shard_map/tok,trk->tro/dot_general | solution.py:19
  250.4 1.5 fusion.2
  (59 shorter events, 16.3 us)
Async XLA Ops:
  7.2 52.4 %copy-start = (bf16[256,32,128]{2,1,0:T(8,128)(2,1)S(1)}, bf16[256,32,128]{2,1,0:T(8,128)(2,1)}, u32[]{:S(2)}) copy-start(bf16[256,32,128]{2,1,0:T(8,128)(2,1)} %param.16) | copy-start | bytes 6291460
  7.2 47.1 %all-gather.4.cloned.1.call-start = ((), (), s32[]{:S(2)}) async-start(), calls=%async_computation.3 | async-start | bytes 1310720 | tf_op jit(solution)/shard_map/all_gather | solution.py:50
  20.1 2.8 %copy-start.5 = (s32[512]{0:T(512)S(1)}, s32[512]{0:T(512)}, u32[]{:S(2)}) copy-start(s32[512]{0:T(512)} %param.14) | copy-start | bytes 6148
  22.9 1.6 copy-start.4
  22.9 2.6 copy-start.7
  22.9 15.5 %copy-start.6 = (s32[256]{0:T(256)S(1)}, s32[256]{0:T(256)}, u32[]{:S(2)}) copy-start(s32[256]{0:T(256)} %param.18) | copy-start | bytes 3076
  26.4 46.3 %all-to-all-start = ((s32[64,1,8]{2,1,0:T(1,128)}), s32[64,1,8]{2,1,0:T(1,128)S(1)}, u32[]{:S(2)}, u32[]{:S(2)}) async-start(s32[64,1,8]{2,1,0:T(1,128)} %bitcast.6), calls=%async_computation | async-start | bytes 65536 | tf_op jit(solution)/shard_map/all_to_all | solution.py:75
  72.6 39.3 %all-to-all-start.1 = ((f32[64,1,4096]{2,1,0:T(1,128)}), f32[64,1,4096]{2,1,0:T(1,128)S(1)}, u32[]{:S(2)}, u32[]{:S(2)}) async-start(f32[64,1,4096]{2,1,0:T(1,128)} %reshape.169), calls=%async_computation.1 | async-start | bytes 2097152 | tf_op jit(solution)/shard_map/all_to_all | solution.py:74
  83.2 116.2 %all-gather.6.cloned.1.call-start = ((), (), s32[]{:S(2)}) async-start(), calls=%async_computation.4 | async-start | bytes 1310720 | tf_op jit(solution)/shard_map/all_gather | solution.py:93
  127.0 1.0 copy-start.3
  127.1 16.3 %copy-start.2 = (bf16[32,32,128]{2,1,0:T(8,128)(2,1)S(1)}, bf16[32,32,128]{2,1,0:T(8,128)(2,1)}, u32[]{:S(2)}) copy-start(bf16[32,32,128]{2,1,0:T(8,128)(2,1)} %param.21) | copy-start | bytes 786436
  177.5 57.8 %all-gather.8.cloned.1.call-start = ((), (), s32[]{:S(2)}) async-start(), calls=%async_computation.5 | async-start | bytes 1310720 | tf_op jit(solution)/shard_map/all_gather | solution.py:96
  247.5 4.4 %copy-start.1 = (bf16[256,32,128]{2,1,0:T(8,128)(2,1)S(1)}, bf16[256,32,128]{2,1,0:T(8,128)(2,1)}, u32[]{:S(2)}) copy-start(bf16[256,32,128]{2,1,0:T(8,128)(2,1)} %param.16) | copy-start | bytes 6291460
Sparse Core Ops, SparseCore 0:
  24.6 29.6 all-gather.3
  177.6 21.7 all-gather.5
  208.2 27.0 all-gather.7
where the time goes:
time: 259 us; the launch traced here: 258 us
  waiting for transfers between devices  91.2 us (35%)
  local copies, waits for them, and re-layouts  60 us (23%)
  blocking collectives  36.2 us (14%)
  matrix products  28.3 us (11%)
  starting transfers between devices  22.9 us (9%)
  between operations  14.1 us (5%)
  other arithmetic  5.77 us (2%)
    all_to_all x1, waiting for transfers between devices, on_device(): lax.all_to_all(send_values, 'sub', split_axis=0, concat_axis=0, tiled=True)  27.1 us
    all_gather x1, waiting for transfers between devices, on_device(): update_full = lax.all_gather(update_low, 'harm', axis=2, tiled=True)  26.3 us
    all_to_all x1, blocking collectives, on_device(): lax.all_to_all(replies, 'sub', split_axis=0, concat_axis=0, tiled=True)  22.9 us
    all_gather x1, waiting for transfers between devices, on_device(): touch_full = lax.all_gather(touch_low, 'harm', axis=2, tiled=True)  21.9 us
    dot_general x3, matrix products, tile_product(): jnp.einsum('tok,trk->tro', tile_set, columns, preferred_element_type=jnp....  16.9 us
    unnamed x22, local copies, waits for them, and re-layouts  15.9 us
    all_gather x1, waiting for transfers between devices, on_device(): first_full = lax.all_gather(first_pass, 'harm', axis=2, tiled=True)  15.9 us
    all_gather x1, blocking collectives, on_device(): residual_full = lax.all_gather(residual_low, 'harm', axis=2, tiled=True)  13.3 us
  transfers between devices with their start and end apart: 5, of which 4 were waited for; matrix products, arithmetic and copies ran while one was open for 8% of the time, Pallas kernels for 0%

commit v1 on v0

--- a/solution.py
+++ b/solution.py
@@ -2,6 +2,19 @@
 import jax.numpy as jnp
 from jax import lax
 from jax.sharding import PartitionSpec as P
+
+
+def collect_2(value, axis, dim):
+    ways = lax.axis_size(axis)
+    up = [(d, (d + 1) % ways) for d in range(ways)]
+    down = [(d, (d - 1) % ways) for d in range(ways)]
+    earlier, later = ([value], [value])
+    for _ in range(ways // 2):
+        earlier.append(lax.ppermute(earlier[-1], axis, up))
+    for _ in range((ways - 1) // 2):
+        later.append(lax.ppermute(later[-1], axis, down))
+    line = jnp.concatenate([*earlier[::-1], *later[1:]], axis=dim)
+    return jnp.roll(line, (lax.axis_index(axis) - ways // 2) * value.shape[dim], axis=dim)
 
 
 def collect(values, targets, row_total, first_row=0):
@@ -78,7 +91,7 @@
         arrived.reshape((sub_count * capacity,) + value_shape), arrived_rows.reshape(-1), row_count
     )
     residual_low = (own_border - incoming).astype(jnp.bfloat16)
-    residual_full = lax.all_gather(residual_low, "harm", axis=2, tiled=True)
+    residual_full = collect_2(residual_low, "harm", 2)
     solved = jnp.einsum(
         "bok,brk->bro", border_inverse, residual_full, preferred_element_type=jnp.float32
     )

time: 259 us -> 257 us (level)
  blocking collectives: 36.2 us -> 23.3 us
  waiting for transfers between devices: 91.2 us -> 99.3 us
  starting transfers between devices: 22.9 us -> 26.2 us
    all_gather x1 -> x0, blocking collectives: 13.3 us -> none  [on_device(): residual_full = lax.all_gather(residual_low, 'harm', axis=2, tiled=True)]
    ppermute x0 -> x3, waiting for transfers between devices: none -> 8.93 us  [the longest x2 8.92 us: collect_2(): earlier.append(lax.ppermute(earlier[-1], axis, up))]
    ppermute x0 -> x3, starting transfers between devices: none -> 3.39 us  [the longest x1 3 us: collect_2(): later.append(lax.ppermute(later[-1], axis, down))]
    unnamed x22 -> x24, local copies, waits for them, and re-layouts: 15.9 us -> 16 us
  transfers between devices with their start and end apart: 5 -> 8, of which waited for: 4 -> 6; matrix products, arithmetic and copies ran while one was open for 8% -> 8% of each run, Pallas kernels for 0% -> 0%
where the time goes in v1:
time: 257 us; the launch traced here: 256 us
  waiting for transfers between devices  99.3 us (39%)
  local copies, waits for them, and re-layouts  60.1 us (23%)
  matrix products  28.3 us (11%)
  starting transfers between devices  26.2 us (10%)
  blocking collectives  23.3 us (9%)
  between operations  14.1 us (5%)
  other arithmetic  4.95 us (2%)
    all_to_all x1, waiting for transfers between devices, on_device(): lax.all_to_all(send_values, 'sub', split_axis=0, concat_axis=0, tiled=True)  27.2 us
    all_gather x1, waiting for transfers between devices, on_device(): update_full = lax.all_gather(update_low, 'harm', axis=2, tiled=True)  26.3 us
    all_to_all x1, blocking collectives, on_device(): lax.all_to_all(replies, 'sub', split_axis=0, concat_axis=0, tiled=True)  23.3 us
    all_gather x1, waiting for transfers between devices, on_device(): touch_full = lax.all_gather(touch_low, 'harm', axis=2, tiled=True)  20.9 us
    dot_general x3, matrix products, tile_product(): jnp.einsum('tok,trk->tro', tile_set, columns, preferred_element_type=jnp....  16.9 us
    unnamed x24, local copies, waits for them, and re-layouts  16 us
    all_gather x1, waiting for transfers between devices, on_device(): first_full = lax.all_gather(first_pass, 'harm', axis=2, tiled=True)  15.9 us
    all_to_all x1, starting transfers between devices, on_device(): lax.all_to_all(send_rows, 'sub', split_axis=0, concat_axis=0, tiled=True)  12 us
  transfers between devices with their start and end apart: 8, of which 6 were waited for; matrix products, arithmetic and copies ran while one was open for 8% of the time, Pallas kernels for 0%

profile of v1, /device:TPU:2, one launch (start us, length us, event | category | flops | bytes accessed | tf_op | source)
XLA Modules:
  0.0 256.3 jit_solution(16846532182387009536)
XLA Ops:
  7.2 2.4 copy.70
  9.6 2.7 %gather_fusion = bf16[512,16,128]{2,1,0:T(8,128)(2,1)} fusion(bf16[256,16,128]{2,1,0:T(8,128)(2,1)S(1)} %bitcast.105, s32[1024]{0:T(1024)S(1)} %pad_clamp_fusion.2), kind=kCustom, calls=%fused_computation | custom fusion | bytes 4196352 | tf_op jit(solution)/shard_map/gather | solution.py:60
  12.4 7.1 %fusion.36 = f32[512,16,32]{2,1,0:T(8,128)} fusion(bf16[512,16,128]{2,1,0:T(8,128)(2,1)} %gather_fusion, bf16[512,32,128]{2,1,0:T(8,128)(2,1)} %param.13), kind=kOutput, calls=%fused_computation.56 | convolution fusion | flops 67108864 | bytes 7340032 | tf_op jit(solution)/shard_map/tok,trk->tro/dot_general | solution.py:32
  19.4 2.8 %copy.71 = f32[512,16,32]{0,2,1:T(8,128)S(1)} copy(f32[512,16,32]{2,1,0:T(8,128)} %fusion.36) | data formatting | bytes 2097152 | tf_op jit(solution)/shard_map/tok,trk->tro/dot_general | solution.py:32
  25.7 12.0 %all-to-all-start = ((s32[64,1,8]{2,1,0:T(1,128)}), s32[64,1,8]{2,1,0:T(1,128)S(1)}, u32[]{:S(2)}, u32[]{:S(2)}) async-start(s32[64,1,8]{2,1,0:T(1,128)} %bitcast.6), calls=%async_computation | async-start | bytes 65536 | tf_op jit(solution)/shard_map/all_to_all | solution.py:88
  37.8 15.9 %all-gather.4.cloned.1.call-done = bf16[256,16,128]{0,1,2:T(8,128)(2,1)} async-done(((bf16[256,16,32]{0,1,2:T(8,128)(2,1)}), bf16[256,16,128]{0,1,2:T(8,128)(2,1)}) %all-gather.4.cloned.1.call-update) | async-done | bytes 1048592 | tf_op jit(solution)/shard_map/all_gather | solution.py:63
  53.6 3.2 %copy.73 = bf16[256,16,128]{2,1,0:T(8,128)(2,1)} copy(bf16[256,16,128]{0,1,2:T(8,128)(2,1)} %all-gather.4.cloned.1.call-done) | data formatting | bytes 2097152 | tf_op jit(solution)/shard_map/all_gather | solution.py:63
  56.8 2.1 gather_fusion.1
  58.9 2.5 fusion.37
  61.4 2.5 copy.74
  63.9 3.4 %fusion.31 = f32[64,16,8,32]{3,2,1,0:T(8,128)} fusion(f32[256,16,32]{0,2,1:T(8,128)S(1)} %copy.74, s32[256]{0:T(256)S(1)} %multiply_add_fusion.1, s32[64,8]{1,0:T(8,128)S(1)} %multiply_add_fusion), kind=kOutput, calls=%fused_computation.55 | convolution fusion | flops 805437440 | bytes 1575936 | tf_op jit(solution)/shard_map/dot_general | solution.py:77
  67.3 4.7 %reshape.169 = f32[64,1,4096]{2,1,0:T(1,128)} reshape(f32[64,16,8,32]{3,2,1,0:T(8,128)} %fusion.31) | data formatting | bytes 2097152
  72.0 10.5 %all-to-all-start.1 = ((f32[64,1,4096]{2,1,0:T(1,128)}), f32[64,1,4096]{2,1,0:T(1,128)S(1)}, u32[]{:S(2)}, u32[]{:S(2)}) async-start(f32[64,1,4096]{2,1,0:T(1,128)} %reshape.169), calls=%async_computation.1 | async-start | bytes 2097152 | tf_op jit(solution)/shard_map/all_to_all | solution.py:87
  84.1 27.2 %all-to-all-done.1 = f32[64,1,4096]{2,1,0:T(1,128)S(1)} async-done(((f32[64,1,4096]{2,1,0:T(1,128)}), f32[64,1,4096]{2,1,0:T(1,128)S(1)}, u32[]{:S(2)}, u32[]{:S(2)}) %all-to-all-start.1) | async-done | bytes 1048608 | tf_op jit(solution)/shard_map/all_to_all | solution.py:87
  111.8 3.3 %reduce.6 = f32[64,4096]{1,0:T(8,128)S(1)} reduce(f32[64,1,4096]{2,1,0:T(1,128)S(1)} %all-to-all-done.1, f32[]{:T(128)} %broadcast.93), dimensions={1}, to_apply=%all_to_all.16.reduce_sub_computation | reduce | bytes 2097156 | tf_op jit(solution)/shard_map/all_to_all | solution.py:87
  115.1 2.7 %reshape.170 = f32[64,16,8,32]{3,2,1,0:T(8,128)} reshape(f32[64,4096]{1,0:T(8,128)S(1)} %reduce.6) | data formatting | bytes 2097152
  117.8 5.1 %copy.75 = f32[64,8,16,32]{3,2,1,0:T(8,128)} copy(f32[64,8,16,32]{3,1,2,0:T(8,128)} %bitcast.104) | data formatting | bytes 2097152 | tf_op jit(solution)/shard_map/all_to_all | solution.py:87
  122.8 3.5 %reshape_reshape.3 = f32[512,512]{1,0:T(8,128)S(1)} reshape(f32[64,8,16,32]{3,2,1,0:T(8,128)} %copy.75) | data formatting | bytes 2097152 | tf_op jit(solution)/shard_map/reshape;reshape | solution.py:24
  129.2 3.0 %collective-permute-start.2 = (bf16[32,16,32]{2,0,1:T(8,128)(2,1)S(1)}, bf16[32,16,32]{2,0,1:T(8,128)(2,1)S(1)}, u32[]{:S(2)}, u32[]{:S(2)}) collective-permute-start(bf16[32,16,32]{2,0,1:T(8,128)(2,1)S(1)} %fusion.1), channel_id=1, source_target_pairs={{0,3},{1,0},{2,1},{3,2},{4,7},{5,4},{6,5},{7,6},{8,11},{9,8},{10,9... | collective-permute-start | bytes 98312 | tf_op jit(solution)/shard_map/ppermute | solution.py:15
  132.2 2.8 %collective-permute-done = bf16[32,16,32]{2,0,1:T(8,128)(2,1)S(1)} collective-permute-done((bf16[32,16,32]{2,0,1:T(8,128)(2,1)S(1)}, bf16[32,16,32]{2,0,1:T(8,128)(2,1)S(1)}, u32[]{:S(2)}, u32[]{:S(2)}) %collective-permute-start) | collective-permute-done | bytes 32800 | tf_op jit(solution)/shard_map/ppermute | solution.py:13
  135.0 6.2 %collective-permute-done.1 = bf16[32,16,32]{2,0,1:T(8,128)(2,1)S(1)} collective-permute-done((bf16[32,16,32]{2,0,1:T(8,128)(2,1)S(1)}, bf16[32,16,32]{2,0,1:T(8,128)(2,1)S(1)}, u32[]{:S(2)}, u32[]{:S(2)}) %collective-permute-start.1) | collective-permute-done | bytes 32800 | tf_op jit(solution)/shard_map/ppermute | solution.py:13
  142.0 2.8 %gather_fusion.2 = bf16[512,16,32]{2,1,0:T(8,128)(2,1)} fusion(bf16[32,16,32]{2,1,0:T(8,128)(2,1)S(1)} %get-tuple-element.12, s32[1024]{0:T(1024)S(1)} %pad_clamp_fusion), kind=kCustom, calls=%fused_computation.2 | custom fusion | bytes 1050624 | tf_op jit(solution)/shard_map/gather | solution.py:99
  144.8 3.7 %reshape.171 = bf16[64,2,2048]{2,1,0:T(2,128)(2,1)S(1)} reshape(bf16[64,8,16,32]{3,2,1,0:T(8,128)(2,1)} %bitcast.106) | data formatting | bytes 1048576
  148.5 23.3 %all_to_all.22 = bf16[64,2,2048]{2,1,0:T(2,128)(2,1)S(1)} all-to-all(bf16[64,2,2048]{2,1,0:T(2,128)(2,1)S(1)} %reshape.171), channel_id=1, replica_groups=mesh['sub'=64,'harm'=4] {'sub'}, dimensions={0} | all-to-all | bytes 1048576 | tf_op jit(solution)/shard_map/all_to_all | solution.py:100
  176.3 20.9 %all-gather.6.cloned.1.call-done = bf16[256,16,128]{0,1,2:T(8,128)(2,1)} async-done(((bf16[256,16,32]{0,1,2:T(8,128)(2,1)}), bf16[256,16,128]{0,1,2:T(8,128)(2,1)}) %all-gather.6.cloned.1.call-update) | async-done | bytes 1048592 | tf_op jit(solution)/shard_map/all_gather | solution.py:106
  197.2 2.5 copy.80
  199.7 2.8 %fusion.38 = f32[256,16,32]{2,1,0:T(8,128)S(1)} fusion(bf16[256,16,128]{2,1,0:T(8,128)(2,1)S(1)} %copy.80, bf16[256,32,128]{2,1,0:T(8,128)(2,1)} %param.17), kind=kOutput, calls=%fused_computation.58 | convolution fusion | flops 33554432 | bytes 3670016 | tf_op jit(solution)/shard_map/tok,trk->tro/dot_general | solution.py:32
  206.7 26.3 %all-gather.8.cloned.1.call-done = bf16[256,16,128]{0,1,2:T(8,128)(2,1)} async-done(((bf16[256,16,32]{0,1,2:T(8,128)(2,1)}), bf16[256,16,128]{0,1,2:T(8,128)(2,1)}) %all-gather.8.cloned.1.call-update) | async-done | bytes 1048592 | tf_op jit(solution)/shard_map/all_gather | solution.py:109
  233.1 2.5 copy.83
  235.5 2.7 %gather_fusion.3 = bf16[512,16,128]{2,1,0:T(8,128)(2,1)} fusion(bf16[256,16,128]{2,1,0:T(8,128)(2,1)S(1)} %copy.83, s32[1024]{0:T(1024)S(1)} %pad_clamp_fusion.2), kind=kCustom, calls=%fused_computation.3 | custom fusion | bytes 4196352 | tf_op jit(solution)/shard_map/gather | solution.py:110
  238.3 7.1 %fusion.39 = f32[512,16,32]{2,1,0:T(8,128)} fusion(bf16[512,16,128]{2,1,0:T(8,128)(2,1)} %gather_fusion.3, bf16[512,32,128]{2,1,0:T(8,128)(2,1)} %param.13), kind=kOutput, calls=%fused_computation.59 | convolution fusion | flops 67108864 | bytes 7340032 | tf_op jit(solution)/shard_map/tok,trk->tro/dot_general | solution.py:32
  245.3 2.9 %copy.84 = f32[512,16,32]{0,2,1:T(8,128)S(1)} copy(f32[512,16,32]{2,1,0:T(8,128)} %fusion.39) | data formatting | bytes 2097152 | tf_op jit(solution)/shard_map/tok,trk->tro/dot_general | solution.py:32
  (66 shorter events, 19.3 us)
Async XLA Ops:
  7.2 51.7 %copy-start = (bf16[256,32,128]{2,1,0:T(8,128)(2,1)S(1)}, bf16[256,32,128]{2,1,0:T(8,128)(2,1)}, u32[]{:S(2)}) copy-start(bf16[256,32,128]{2,1,0:T(8,128)(2,1)} %param.16) | copy-start | bytes 6291460
  7.2 2.4 copy-start.7
  7.2 46.4 %all-gather.4.cloned.1.call-start = ((), (), s32[]{:S(2)}) async-start(), calls=%async_computation.3 | async-start | bytes 1310720 | tf_op jit(solution)/shard_map/all_gather | solution.py:63
  19.4 2.8 %copy-start.5 = (s32[512]{0:T(512)S(1)}, s32[512]{0:T(512)}, u32[]{:S(2)}) copy-start(s32[512]{0:T(512)} %param.14) | copy-start | bytes 6148
  22.2 1.6 copy-start.4
  22.3 2.6 %copy-start.8 = (s32[256]{0:T(256)S(1)}, s32[256]{0:T(256)}, u32[]{:S(2)}) copy-start(s32[256]{0:T(256)} %param.20) | copy-start | bytes 3076
  22.3 15.5 %copy-start.6 = (s32[256]{0:T(256)S(1)}, s32[256]{0:T(256)}, u32[]{:S(2)}) copy-start(s32[256]{0:T(256)} %param.18) | copy-start | bytes 3076
  25.7 46.3 %all-to-all-start = ((s32[64,1,8]{2,1,0:T(1,128)}), s32[64,1,8]{2,1,0:T(1,128)S(1)}, u32[]{:S(2)}, u32[]{:S(2)}) async-start(s32[64,1,8]{2,1,0:T(1,128)} %bitcast.6), calls=%async_computation | async-start | bytes 65536 | tf_op jit(solution)/shard_map/all_to_all | solution.py:88
  72.0 39.3 %all-to-all-start.1 = ((f32[64,1,4096]{2,1,0:T(1,128)}), f32[64,1,4096]{2,1,0:T(1,128)S(1)}, u32[]{:S(2)}, u32[]{:S(2)}) async-start(f32[64,1,4096]{2,1,0:T(1,128)} %reshape.169), calls=%async_computation.1 | async-start | bytes 2097152 | tf_op jit(solution)/shard_map/all_to_all | solution.py:87
  82.5 114.7 %all-gather.6.cloned.1.call-start = ((), (), s32[]{:S(2)}) async-start(), calls=%async_computation.4 | async-start | bytes 1310720 | tf_op jit(solution)/shard_map/all_gather | solution.py:106
  126.4 1.0 copy-start.3
  126.4 15.3 %copy-start.2 = (bf16[32,32,128]{2,1,0:T(8,128)(2,1)S(1)}, bf16[32,32,128]{2,1,0:T(8,128)(2,1)}, u32[]{:S(2)}) copy-start(bf16[32,32,128]{2,1,0:T(8,128)(2,1)} %param.21) | copy-start | bytes 786436
  128.7 6.3 %collective-permute-start = (bf16[32,16,32]{2,0,1:T(8,128)(2,1)S(1)}, bf16[32,16,32]{2,0,1:T(8,128)(2,1)S(1)}, u32[]{:S(2)}, u32[]{:S(2)}) collective-permute-start(bf16[32,16,32]{2,0,1:T(8,128)(2,1)S(1)} %fusion.1), channel_id=1, source_target_pairs={{0,1},{1,2},{2,3},{3,0},{4,5},{5,6},{6,7},{7,4},{8,9},{9,10},{10,1... | collective-permute-start | bytes 98312 | tf_op jit(solution)/shard_map/ppermute | solution.py:13
  129.2 5.8 %collective-permute-start.2 = (bf16[32,16,32]{2,0,1:T(8,128)(2,1)S(1)}, bf16[32,16,32]{2,0,1:T(8,128)(2,1)S(1)}, u32[]{:S(2)}, u32[]{:S(2)}) collective-permute-start(bf16[32,16,32]{2,0,1:T(8,128)(2,1)S(1)} %fusion.1), channel_id=1, source_target_pairs={{0,3},{1,0},{2,1},{3,2},{4,7},{5,4},{6,5},{7,6},{8,11},{9,8},{10,9... | collective-permute-start | bytes 98312 | tf_op jit(solution)/shard_map/ppermute | solution.py:15
  134.9 6.2 %collective-permute-start.1 = (bf16[32,16,32]{2,0,1:T(8,128)(2,1)S(1)}, bf16[32,16,32]{2,0,1:T(8,128)(2,1)S(1)}, u32[]{:S(2)}, u32[]{:S(2)}) collective-permute-start(bf16[32,16,32]{2,0,1:T(8,128)(2,1)S(1)} %collective-permute-done), channel_id=1, source_target_pairs={{0,1},{1,2},{2,3},{3,0},{4,5},{5,6},{6,7},{7,4},{8,9},{9,10},{10,1... | collective-permute-start | bytes 98312 | tf_op jit(solution)/shard_map/ppermute | solution.py:13
  176.3 56.8 %all-gather.8.cloned.1.call-start = ((), (), s32[]{:S(2)}) async-start(), calls=%async_computation.5 | async-start | bytes 1310720 | tf_op jit(solution)/shard_map/all_gather | solution.py:109
  245.3 4.4 %copy-start.1 = (bf16[256,32,128]{2,1,0:T(8,128)(2,1)S(1)}, bf16[256,32,128]{2,1,0:T(8,128)(2,1)}, u32[]{:S(2)}) copy-start(bf16[256,32,128]{2,1,0:T(8,128)(2,1)} %param.16) | copy-start | bytes 6291460
Sparse Core Ops, SparseCore 0:
  24.0 29.6 all-gather.3
  176.4 20.8 all-gather.5
  206.0 27.0 all-gather.7
